TPU v7x, 32 devices: a whole 2x2x4 slice. The times are simulated.
32 devices in a mesh: section: 4 (over y, core), expert: 8 (over z, x).
Axes of the slice: x: 2, y: 2, z: 4, core: 2. Of those that a mesh axis runs over, the one named last changes fastest.
Arguments:
- upstream: bfloat16 [4, 1024, 2048], P('section', 'expert'), may hold values from -6 to 6
- layer_input: bfloat16 [4, 1024, 2048], P('section', 'expert'), may hold values from -6 to 6
- routes: int32 [4, 1024, 2], P('section', 'expert'), may hold values from 0 to 3, all different within a row; in each aligned block of 128 rows (0 to 127, 128 to 255, ..., all dimensions but the last counted through in order) at most 128 rows name the same one
- gate_units: int32 [4, 1024, 2], P('section', 'expert'), may hold values from 1 to 256
- gate_weight: bfloat16 [4, 2048, 3072], P('section', None, 'expert'), may hold values from -0.125 to 0.125
- up_weight: bfloat16 [4, 2048, 3072], P('section', None, 'expert'), may hold values from -0.125 to 0.125
- down_weight: bfloat16 [4, 3072, 2048], P('section', 'expert'), may hold values from -0.21875 to 0.21875
Outputs:
- grad_input: bfloat16 [4, 1024, 2048], P('section', 'expert')
- grad_gate: bfloat16 [4, 2048, 3072], P('section', None, 'expert')
- grad_up: bfloat16 [4, 2048, 3072], P('section', None, 'expert')
- grad_down: bfloat16 [4, 3072, 2048], P('section', 'expert')
Inputs may be any that keep to these rules, and one draw needn't show every extreme that they name: `routes`: each token names 2 different experts; in each block of 128 tokens of a section (the tokens of one device) at most 128 tokens name one expert, and in some block exactly 128 do.
All inputs are finite; a program needn't handle non-finite values.
Results may differ from a plain program's by a relative error of at most 0.0058.
Values may be sent and summed in bfloat16 or wider, within the bound.
No kernel may reach another device: no remote copies, remote signals or barrier semaphores. Data moves between devices by JAX's collectives and lax.ppermute only.
A program may use at most 128 MiB of HBM per device.

v0:
```python
import jax
import jax.numpy as jnp
from jax import lax
from jax.sharding import PartitionSpec as P


def passed_along(value, axis, steps):
    count = lax.axis_size(axis)
    pairs = [(source, (source + steps) % count) for source in range(count)]
    return lax.ppermute(value, axis, pairs)


def expert_half(inputs, grads, w_gate, w_up, w_down):
    gate = jnp.dot(inputs, w_gate, preferred_element_type=jnp.float32)
    upper = jnp.dot(inputs, w_up, preferred_element_type=jnp.float32)
    sig = jax.nn.sigmoid(gate)
    act = gate * sig
    hidden = (act * upper).astype(jnp.bfloat16)
    dact = lax.dot_general(
        grads, w_down, (((1,), (1,)), ((), ())), preferred_element_type=jnp.float32
    )
    d_up = (dact * act).astype(jnp.bfloat16)
    d_gate = (dact * upper * sig * (1.0 + gate * (1.0 - sig))).astype(jnp.bfloat16)
    inner = (((1,), (1,)), ((), ()))
    d_in = lax.dot_general(d_gate, w_gate, inner, preferred_element_type=jnp.float32)
    d_in = d_in + lax.dot_general(d_up, w_up, inner, preferred_element_type=jnp.float32)
    outer = (((0,), (0,)), ((), ()))
    g_down = lax.dot_general(hidden, grads, outer, preferred_element_type=jnp.float32).astype(
        jnp.bfloat16
    )
    g_gate = lax.dot_general(inputs, d_gate, outer, preferred_element_type=jnp.float32).astype(
        jnp.bfloat16
    )
    g_up = lax.dot_general(inputs, d_up, outer, preferred_element_type=jnp.float32).astype(
        jnp.bfloat16
    )
    return (d_in.astype(jnp.bfloat16), g_gate, g_up, g_down)


def shards(upstream, layer_input, routes, gate_units, gate_weight, up_weight, down_weight):
    received = passed_along(upstream, "section", -1)[0]
    tokens = layer_input[0]
    expert = lax.axis_index("expert") // 2
    all_tokens = lax.all_gather(tokens, "expert", axis=0, tiled=True)
    all_grads = lax.all_gather(received, "expert", axis=0, tiled=True)
    all_routes = lax.all_gather(routes[0], "expert", axis=0, tiled=True)
    all_units = lax.all_gather(gate_units[0], "expert", axis=0, tiled=True)
    gains = jnp.sum(
        jnp.where(all_routes == expert, all_units.astype(jnp.float32) / 256.0, 0.0), axis=1
    )
    weighted = (gains[:, None] * all_grads.astype(jnp.float32)).astype(jnp.bfloat16)
    d_in, g_gate, g_up, g_down = expert_half(
        all_tokens, weighted, gate_weight[0], up_weight[0], down_weight[0]
    )
    summed = lax.psum_scatter(d_in.astype(jnp.float32), "expert", scatter_dimension=0, tiled=True)
    grad_input = (summed + received.astype(jnp.float32)).astype(jnp.bfloat16)
    return (grad_input[None], g_gate[None], g_up[None], g_down[None])


def solution(mesh):
    in_specs = (
        P("section", "expert", None),
        P("section", "expert", None),
        P("section", "expert", None),
        P("section", "expert", None),
        P("section", None, "expert"),
        P("section", None, "expert"),
        P("section", "expert", None),
    )
    out_specs = (
        P("section", "expert", None),
        P("section", None, "expert"),
        P("section", None, "expert"),
        P("section", "expert", None),
    )
    return jax.shard_map(shards, mesh=mesh, in_specs=in_specs, out_specs=out_specs, check_vma=False)
```

profile of v0, /device:TPU:0, one launch (start us, length us, event | category | flops | bytes accessed | tf_op | source)
XLA Modules:
  0.0 331.4 jit_solution(4760866613073092125)
XLA Ops:
  7.2 0.0 copy-start
  7.2 0.0 all-gather.9.cloned.1.call-start
  7.2 0.7 all-gather.9.cloned.1.call-update
  7.9 0.0 all-gather.7.cloned.1.call-start
  8.0 2.5 collective-permute-start
  10.4 7.0 %collective-permute-done = bf16[1,128,2048]{2,1,0:T(8,128)(2,1)S(1)} collective-permute-done((bf16[1,128,2048]{2,1,0:T(8,128)(2,1)}, bf16[1,128,2048]{2,1,0:T(8,128)(2,1)S(1)}, u32[]{:S(2)}, u32[]{:S(2)}) %collective-permute-start) | collective-permute-done | bytes 524320 | tf_op jit(solution)/shard_map/ppermute | solution.py:10
  17.4 0.8 copy-done.1
  18.2 0.0 all-gather.7.cloned.1.call-update
  18.3 0.0 reduce-scatter.2.cloned.1.call-start
  18.3 21.2 %all-gather = s32[1,1024,2]{1,2,0:T(2,128)S(1)} all-gather(s32[1,128,2]{1,2,0:T(2,128)} %param.9), channel_id=2, replica_groups=mesh['section'=4,'expert'=8] {'expert'}, dimensions={1}, use_global_device_ids=true | all-gather | bytes 9216 | tf_op jit(solution)/shard_map/all_gather | solution.py:46
  39.6 16.8 %all-gather.1 = s32[1,1024,2]{1,2,0:T(2,128)S(1)} all-gather(s32[1,128,2]{1,2,0:T(2,128)} %param.10), channel_id=3, replica_groups=mesh['section'=4,'expert'=8] {'expert'}, dimensions={1}, use_global_device_ids=true | all-gather | bytes 9216 | tf_op jit(solution)/shard_map/all_gather | solution.py:47
  56.4 0.0 copy-start.3
  56.4 30.0 %all-gather.9.cloned.1.call-done = bf16[1,1024,2048]{2,1,0:T(8,128)(2,1)} async-done(((bf16[1,128,2048]{2,1,0:T(8,128)(2,1)}), bf16[1,1024,2048]{2,1,0:T(8,128)(2,1)}) %all-gather.9.cloned.1.call-update) | async-done | bytes 4194320 | tf_op jit(solution)/shard_map/all_gather | solution.py:44
  86.4 0.0 copy-done
  86.4 5.8 %fusion.5 = f32[1024,384]{1,0:T(8,128)} fusion(bf16[1,1024,2048]{2,1,0:T(8,128)(2,1)} %all-gather.9.cloned.1.call-done, bf16[1,2048,384]{2,1,0:T(8,128)(2,1)S(1)} %copy-done), kind=kOutput, calls=%fused_computation.7 | convolution fusion | flops 1610612736 | bytes 7340032 | tf_op jit(solution)/shard_map/dot_general | solution.py:14
  92.2 0.0 copy-done.3
  92.2 0.0 copy-done.6
  92.2 3.5 %fusion.7 = f32[1024,384]{1,0:T(8,128)} fusion(bf16[1,1024,2048]{2,1,0:T(8,128)(2,1)S(1)} %copy-done.6, bf16[1,2048,384]{2,1,0:T(8,128)(2,1)S(1)} %copy-done.3), kind=kOutput, calls=%fused_computation.9 | convolution fusion | flops 1610612736 | bytes 7340032 | tf_op jit(solution)/shard_map/dot_general | solution.py:15
  95.7 65.1 %all-gather.7.cloned.1.call-done = bf16[1,1024,2048]{2,1,0:T(8,128)(2,1)} async-done(((bf16[1,128,2048]{2,1,0:T(8,128)(2,1)}), bf16[1,1024,2048]{2,1,0:T(8,128)(2,1)}) %all-gather.7.cloned.1.call-update) | async-done | bytes 4194320 | tf_op jit(solution)/shard_map/all_gather | solution.py:45
  160.8 6.4 %multiply_convert_fusion.1 = (bf16[1024,384]{1,0:T(8,128)(2,1)S(1)}, bf16[1024,384]{1,0:T(8,128)(2,1)S(1)}) fusion(f32[1024,384]{1,0:T(8,128)} %fusion.5, f32[1024,384]{1,0:T(8,128)} %fusion.7, bf16[1,384,2048]{2,1,0:T(8,128)(2,1)} %param.13, bf16[1,1024,2048]{2,1,0:T(8,128)(2,1)} %all-gather.7.cloned.1.call-done, f32[1024]{0:T(1024)S(1)} %fusion.36), kind=kOutput, calls=%fused_computation.26 | convolution fusion | flops 1622016000 | bytes 10489856 | tf_op jit(solution)/shard_map/dot_general | solution.py:19
  167.2 0.0 copy-start.4
  167.2 0.0 copy-start.5
  167.2 2.4 fusion.26
  169.6 5.6 %fusion.9 = f32[1024,2048]{1,0:T(8,128)} fusion(f32[1024,2048]{1,0:T(8,128)S(1)} %fusion.26, bf16[1024,384]{1,0:T(8,128)(2,1)S(1)} %get-tuple-element.8, bf16[1,2048,384]{2,1,0:T(8,128)(2,1)S(1)} %copy-done.3), kind=kOutput, calls=%fused_computation.11 | convolution fusion | flops 1616904192 | bytes 19136512 | tf_op jit(solution)/shard_map/dot_general | solution.py:26
  175.2 0.0 reduce-scatter.2.cloned.1.call-update
  175.2 4.3 %fusion.20 = bf16[1,2048,384]{1,2,0:T(8,128)(2,1)S(1)} fusion(bf16[1024,384]{1,0:T(8,128)(2,1)} %copy-done.4, bf16[1,1024,2048]{2,1,0:T(8,128)(2,1)} %all-gather.9.cloned.1.call-done), kind=kOutput, calls=%fused_computation.17 | convolution fusion | flops 1611399168 | bytes 6553600 | tf_op jit(solution)/shard_map/dot_general | solution.py:31
  179.5 1.8 copy.11
  181.3 4.3 %fusion.17 = bf16[1,2048,384]{1,2,0:T(8,128)(2,1)S(1)} fusion(bf16[1024,384]{1,0:T(8,128)(2,1)} %copy-done.5, bf16[1,1024,2048]{2,1,0:T(8,128)(2,1)} %all-gather.9.cloned.1.call-done), kind=kOutput, calls=%fused_computation.16 | convolution fusion | flops 1611399168 | bytes 6553600 | tf_op jit(solution)/shard_map/dot_general | solution.py:34
  185.6 1.6 copy.12
  187.1 6.5 %fusion.16 = bf16[1,384,2048]{2,1,0:T(8,128)(2,1)} fusion(bf16[1,1024,2048]{2,1,0:T(8,128)(2,1)} %all-gather.7.cloned.1.call-done, f32[1024]{0:T(1024)S(1)} %fusion.36, f32[1024,384]{1,0:T(8,128)} %fusion.7, f32[1024,384]{1,0:T(8,128)} %fusion.5), kind=kOutput, calls=%fused_computation.15 | convolution fusion | flops 1620049920 | bytes 8916992 | tf_op jit(solution)/shard_map/dot_general | solution.py:28
  193.6 129.1 %reduce-scatter.2.cloned.1.call-done = f32[128,2048]{1,0:T(8,128)} async-done(((f32[1024,2048]{1,0:T(8,128)}), f32[128,2048]{1,0:T(8,128)}) %reduce-scatter.2.cloned.1.call-update) | async-done | bytes 1048592 | tf_op jit(solution)/shard_map/reduce_scatter | solution.py:55
  322.7 2.1 fusion.34
  (7 shorter events, 0.0 us)
Async XLA Ops:
  7.2 79.2 %copy-start = (bf16[1,2048,384]{2,1,0:T(8,128)(2,1)S(1)}, bf16[1,2048,384]{2,1,0:T(8,128)(2,1)}, u32[]{:S(2)}) copy-start(bf16[1,2048,384]{2,1,0:T(8,128)(2,1)} %param.11) | copy-start | bytes 4718596
  7.2 79.2 %all-gather.9.cloned.1.call-start = ((), (), s32[]{:S(2)}) async-start(), calls=%async_computation.3 | async-start | bytes 4718592 | tf_op jit(solution)/shard_map/all_gather | solution.py:44
  7.9 152.9 %all-gather.7.cloned.1.call-start = ((), (), s32[]{:S(2)}) async-start(), calls=%async_computation.2 | async-start | bytes 4718592 | tf_op jit(solution)/shard_map/all_gather | solution.py:45
  8.0 9.5 %collective-permute-start = (bf16[1,128,2048]{2,1,0:T(8,128)(2,1)}, bf16[1,128,2048]{2,1,0:T(8,128)(2,1)S(1)}, u32[]{:S(2)}, u32[]{:S(2)}) collective-permute-start(bf16[1,128,2048]{2,1,0:T(8,128)(2,1)} %param.7), channel_id=1, source_target_pairs={{0,24},{8,0},{16,8},{24,16},{1,25},{9,1},{17,9},{25,17},{2,26},{10... | collective-permute-start | bytes 1572872 | tf_op jit(solution)/shard_map/ppermute | solution.py:10
  17.4 0.8 copy-start.1
  18.3 304.5 %reduce-scatter.2.cloned.1.call-start = ((), (), s32[]{:S(2)}) async-start(), calls=%async_computation.1 | async-start | bytes 9437184 | tf_op jit(solution)/shard_map/reduce_scatter | solution.py:55
  56.4 35.9 %copy-start.3 = (bf16[1,2048,384]{2,1,0:T(8,128)(2,1)S(1)}, bf16[1,2048,384]{2,1,0:T(8,128)(2,1)}, u32[]{:S(2)}) copy-start(bf16[1,2048,384]{2,1,0:T(8,128)(2,1)} %param.12) | copy-start | bytes 4718596
  86.4 5.8 %copy-start.6 = (bf16[1,1024,2048]{2,1,0:T(8,128)(2,1)S(1)}, bf16[1,1024,2048]{2,1,0:T(8,128)(2,1)}, u32[]{:S(2)}) copy-start(bf16[1,1024,2048]{2,1,0:T(8,128)(2,1)} %all-gather.9.cloned.1.call-done) | copy-start | bytes 12582916
  167.2 2.4 copy-start.4
  167.2 2.4 copy-start.5
  187.1 135.6 %copy-start.2 = (bf16[1,128,2048]{2,1,0:T(8,128)(2,1)S(1)}, bf16[1,128,2048]{2,1,0:T(8,128)(2,1)}, u32[]{:S(2)}) copy-start(bf16[1,128,2048]{2,1,0:T(8,128)(2,1)} %copy-done.1) | copy-start | bytes 1572868
Sparse Core Ops, SparseCore 0:
  10.1 76.2 all-gather.8
  89.1 71.6 all-gather.6
  175.4 147.3 reduce-scatter.1
where the time goes:
time: 332 us; the launch traced here: 331 us
  waiting for transfers between devices  232 us (70%)
  matrix products  38.7 us (12%)
  blocking collectives  38 us (11%)
  between operations  13.8 us (4%)
  local copies, waits for them, and re-layouts  4.15 us (1%)
    reduce_scatter x1, waiting for transfers between devices, shards(): lax.psum_scatter(d_in.astype(jnp.float32), 'expert', scatter_dimension=0,...  129 us
    all_gather x1, waiting for transfers between devices, shards(): all_grads = lax.all_gather(received, 'expert', axis=0, tiled=True)  65.1 us
    all_gather x1, waiting for transfers between devices, shards(): all_tokens = lax.all_gather(tokens, 'expert', axis=0, tiled=True)  30 us
    all_gather x1, blocking collectives, shards(): all_routes = lax.all_gather(routes[0], 'expert', axis=0, tiled=True)  21.2 us
    all_gather x1, blocking collectives, shards(): all_units = lax.all_gather(gate_units[0], 'expert', axis=0, tiled=True)  16.8 us
    ppermute x1, waiting for transfers between devices, passed_along(): return lax.ppermute(value, axis, pairs)  7.02 us
  transfers between devices with their start and end apart: 4, of which 4 were waited for; matrix products, arithmetic and copies ran while one was open for 8% of the time, Pallas kernels for 0%

commit v1 on v0

--- a/solution.py
+++ b/solution.py
@@ -41,8 +41,11 @@
     received = passed_along(upstream, "section", -1)[0]
     tokens = layer_input[0]
     expert = lax.axis_index("expert") // 2
-    all_tokens = lax.all_gather(tokens, "expert", axis=0, tiled=True)
-    all_grads = lax.all_gather(received, "expert", axis=0, tiled=True)
+    all_tokens, all_grads = jnp.split(
+        lax.all_gather(jnp.concatenate([tokens, received], axis=1), "expert", tiled=True, axis=0),
+        [tokens.shape[1]],
+        axis=1,
+    )
     all_routes = lax.all_gather(routes[0], "expert", axis=0, tiled=True)
     all_units = lax.all_gather(gate_units[0], "expert", axis=0, tiled=True)
     gains = jnp.sum(

time: 332 us -> 321 us (0.967)
  matrix products: 38.7 us -> 33.3 us
  waiting for transfers between devices: 232 us -> 228 us
  local copies, waits for them, and re-layouts: 4.15 us -> 0.52 us
    all_gather x2 -> x1, waiting for transfers between devices: 95.1 us -> 89 us  [shards(): lax.all_gather(jnp.concatenate([tokens, received], axis=1), 'expert', til...]
    unnamed x16 -> x26, local copies, waits for them, and re-layouts: 4.15 us -> 0.52 us
    dot_general x1, matrix products: 6.38 us -> 2.9 us  [expert_half(): lax.dot_general(grads, w_down, (((1,), (1,)), ((), ())), preferred_elemen...]
  transfers between devices with their start and end apart: 4 -> 3, of which waited for: 4 -> 3; matrix products, arithmetic and copies ran while one was open for 8% -> 5% of each run, Pallas kernels for 0% -> 0%
where the time goes in v1:
time: 321 us; the launch traced here: 320 us
  waiting for transfers between devices  228 us (71%)
  blocking collectives  37.7 us (12%)
  matrix products  33.3 us (10%)
  between operations  14.2 us (4%)
  other arithmetic  4.28 us (1%)
    reduce_scatter x1, waiting for transfers between devices, shards(): lax.psum_scatter(d_in.astype(jnp.float32), 'expert', scatter_dimension=0,...  132 us
    all_gather x1, waiting for transfers between devices, shards(): lax.all_gather(jnp.concatenate([tokens, received], axis=1), 'expert', til...  89 us
    all_gather x1, blocking collectives, shards(): all_routes = lax.all_gather(routes[0], 'expert', axis=0, tiled=True)  21 us
    all_gather x1, blocking collectives, shards(): all_units = lax.all_gather(gate_units[0], 'expert', axis=0, tiled=True)  16.6 us
    ppermute x1, waiting for transfers between devices, passed_along(): return lax.ppermute(value, axis, pairs)  7.02 us
  transfers between devices with their start and end apart: 3, of which 3 were waited for; matrix products, arithmetic and copies ran while one was open for 5% of the time, Pallas kernels for 0%

profile of v1, /device:TPU:0, one launch (start us, length us, event | category | flops | bytes accessed | tf_op | source)
XLA Modules:
  0.0 320.4 jit_solution(10513925205494376032)
XLA Ops:
  7.2 0.0 copy-start
  7.2 0.0 all-gather.4.cloned.1.call-start
  7.2 2.5 collective-permute-start
  9.7 7.0 %collective-permute-done = bf16[1,128,2048]{2,1,0:T(8,128)(2,1)S(1)} collective-permute-done((bf16[1,128,2048]{2,1,0:T(8,128)(2,1)}, bf16[1,128,2048]{2,1,0:T(8,128)(2,1)S(1)}, u32[]{:S(2)}, u32[]{:S(2)}) %collective-permute-start) | collective-permute-done | bytes 524320 | tf_op jit(solution)/shard_map/ppermute | solution.py:10
  16.7 2.1 pad_maximum_fusion
  18.8 0.0 all-gather.4.cloned.1.call-update
  18.9 0.0 reduce-scatter.2.cloned.1.call-start
  18.9 0.0 copy-done.3
  18.9 21.0 %all-gather = s32[1,1024,2]{1,2,0:T(2,128)S(1)} all-gather(s32[1,128,2]{1,2,0:T(2,128)S(1)} %copy-done.3), channel_id=2, replica_groups=mesh['section'=4,'expert'=8] {'expert'}, dimensions={1}, use_global_device_ids=true | all-gather | bytes 9216 | tf_op jit(solution)/shard_map/all_gather | solution.py:49
  39.9 0.0 copy-done.4
  40.0 16.6 %all-gather.1 = s32[1,1024,2]{1,2,0:T(2,128)S(1)} all-gather(s32[1,128,2]{1,2,0:T(2,128)S(1)} %copy-done.4), channel_id=3, replica_groups=mesh['section'=4,'expert'=8] {'expert'}, dimensions={1}, use_global_device_ids=true | all-gather | bytes 9216 | tf_op jit(solution)/shard_map/all_gather | solution.py:50
  56.6 89.0 %all-gather.4.cloned.1.call-done = bf16[1024,4096]{1,0:T(8,128)(2,1)} async-done(((bf16[128,4096]{1,0:T(8,128)(2,1)}), bf16[1024,4096]{1,0:T(8,128)(2,1)}) %all-gather.4.cloned.1.call-update) | async-done | bytes 8388624 | tf_op jit(solution)/shard_map/all_gather | solution.py:45
  145.6 0.0 copy-done
  145.6 4.7 %fusion.3 = f32[1024,384]{1,0:T(8,128)S(1)} fusion(bf16[1024,4096]{1,0:T(8,128)(2,1)} %all-gather.4.cloned.1.call-done, bf16[1,2048,384]{2,1,0:T(8,128)(2,1)S(1)} %copy-done), kind=kOutput, calls=%fused_computation.8 | convolution fusion | flops 1610612736 | bytes 7340032 | tf_op jit(solution)/shard_map/dot_general | solution.py:14
  150.3 0.0 copy-done.1
  150.3 0.5 copy-done.5
  150.8 2.3 fusion.5
  153.1 0.0 copy-start.9
  153.1 2.9 multiply_convert_fusion.2
  156.0 0.0 copy-done.9
  156.0 0.0 copy-start.2
  156.0 2.4 fusion.14
  158.4 0.0 copy-done.2
  158.4 5.6 %fusion = f32[1024,2048]{1,0:T(8,128)} fusion(f32[1024,2048]{1,0:T(8,128)S(1)} %fusion.14, bf16[1024,384]{1,0:T(8,128)(2,1)S(1)} %get-tuple-element.4, bf16[1,2048,384]{2,1,0:T(8,128)(2,1)S(1)} %copy-done.1), kind=kOutput, calls=%fused_computation.2 | convolution fusion | flops 1616904192 | bytes 19136512 | tf_op jit(solution)/shard_map/dot_general | solution.py:26
  164.0 0.0 reduce-scatter.2.cloned.1.call-update
  164.1 0.0 slice-start
  164.1 6.1 %fusion.10 = bf16[1,2048,384]{2,1,0:T(8,128)(2,1)} fusion(bf16[1024,384]{1,0:T(8,128)(2,1)} %copy-done.2, bf16[1024,4096]{1,0:T(8,128)(2,1)} %all-gather.4.cloned.1.call-done), kind=kOutput, calls=%fused_computation.13 | convolution fusion | flops 1611399168 | bytes 6553600 | tf_op jit(solution)/shard_map/dot_general | solution.py:34
  170.2 6.1 %fusion.7 = bf16[1,2048,384]{2,1,0:T(8,128)(2,1)} fusion(bf16[1024,384]{1,0:T(8,128)(2,1)S(1)} %get-tuple-element.5, bf16[1024,4096]{1,0:T(8,128)(2,1)} %all-gather.4.cloned.1.call-done), kind=kOutput, calls=%fused_computation.12 | convolution fusion | flops 1611399168 | bytes 6553600 | tf_op jit(solution)/shard_map/dot_general | solution.py:31
  176.3 0.0 slice-done.1
  176.3 3.2 %fusion.13 = bf16[1,384,2048]{2,1,0:T(8,128)(2,1)} fusion(bf16[1024,4096]{1,0:T(8,128)(2,1)S(1)} %bitcast.33, f32[1024]{0:T(1024)S(1)} %fusion.24, f32[1024,384]{1,0:T(8,128)S(1)} %copy-done.10, f32[1024,384]{1,0:T(8,128)S(1)} %copy-done.8), kind=kOutput, calls=%fused_computation.14 | convolution fusion | flops 1620049920 | bytes 8916992 | tf_op jit(solution)/shard_map/dot_general | solution.py:28
  179.5 131.9 %reduce-scatter.2.cloned.1.call-done = f32[128,2048]{1,0:T(8,128)} async-done(((f32[1024,2048]{1,0:T(8,128)}), f32[128,2048]{1,0:T(8,128)}) %reduce-scatter.2.cloned.1.call-update) | async-done | bytes 1048592 | tf_op jit(solution)/shard_map/reduce_scatter | solution.py:58
  311.4 2.1 fusion.22
  (16 shorter events, 0.0 us)
Async XLA Ops:
  7.2 138.4 %copy-start = (bf16[1,2048,384]{2,1,0:T(8,128)(2,1)S(1)}, bf16[1,2048,384]{2,1,0:T(8,128)(2,1)}, u32[]{:S(2)}) copy-start(bf16[1,2048,384]{2,1,0:T(8,128)(2,1)} %param.11) | copy-start | bytes 4718596
  7.2 138.4 %all-gather.4.cloned.1.call-start = ((), (), s32[]{:S(2)}) async-start(), calls=%async_computation.1 | async-start | bytes 9437184 | tf_op jit(solution)/shard_map/all_gather | solution.py:45
  7.2 9.5 %collective-permute-start = (bf16[1,128,2048]{2,1,0:T(8,128)(2,1)}, bf16[1,128,2048]{2,1,0:T(8,128)(2,1)S(1)}, u32[]{:S(2)}, u32[]{:S(2)}) collective-permute-start(bf16[1,128,2048]{2,1,0:T(8,128)(2,1)} %param.7), channel_id=1, source_target_pairs={{0,24},{8,0},{16,8},{24,16},{1,25},{9,1},{17,9},{25,17},{2,26},{10... | collective-permute-start | bytes 1572872 | tf_op jit(solution)/shard_map/ppermute | solution.py:10
  16.7 2.2 copy-start.3
  16.7 23.2 %copy-start.4 = (s32[1,128,2]{1,2,0:T(2,128)S(1)}, s32[1,128,2]{1,2,0:T(2,128)}, u32[]{:S(2)}) copy-start(s32[1,128,2]{1,2,0:T(2,128)} %param.10) | copy-start | bytes 3076
  18.9 292.6 %reduce-scatter.2.cloned.1.call-start = ((), (), s32[]{:S(2)}) async-start(), calls=%async_computation.2 | async-start | bytes 9437184 | tf_op jit(solution)/shard_map/reduce_scatter | solution.py:58
  145.6 4.7 %copy-start.1 = (bf16[1,2048,384]{2,1,0:T(8,128)(2,1)S(1)}, bf16[1,2048,384]{2,1,0:T(8,128)(2,1)}, u32[]{:S(2)}) copy-start(bf16[1,2048,384]{2,1,0:T(8,128)(2,1)} %param.12) | copy-start | bytes 4718596
  145.6 5.1 %copy-start.5 = (bf16[1024,4096]{1,0:T(8,128)(2,1)S(1)}, bf16[1024,4096]{1,0:T(8,128)(2,1)}, u32[]{:S(2)}) copy-start(bf16[1024,4096]{1,0:T(8,128)(2,1)} %all-gather.4.cloned.1.call-done) | copy-start | bytes 25165828
  150.7 2.3 copy-start.7
  150.7 2.3 copy-start.6
  153.1 2.9 copy-start.9
  156.0 2.4 copy-start.2
  164.1 12.2 %slice-start = ((s8[8388608]{0:T(1024)(128)(4,1)}), s8[4194304]{0:T(1024)(128)(4,1)S(1)}, s32[]{:S(2)}) async-start(s8[8388608]{0:T(1024)(128)(4,1)} %bitcast.32), calls=%async_computation.3 | async-start | bytes 8388608
  170.2 6.1 %slice-start.1 = ((s8[8388608]{0:T(1024)(128)(4,1)}), s8[4194304]{0:T(1024)(128)(4,1)S(1)}, s32[]{:S(2)}) async-start(s8[8388608]{0:T(1024)(128)(4,1)} %bitcast.32), calls=%async_computation.4 | async-start | bytes 8388608
  170.2 6.1 %copy-start.8 = (f32[1024,384]{1,0:T(8,128)S(1)}, f32[1024,384]{1,0:T(8,128)}, u32[]{:S(2)}) copy-start(f32[1024,384]{1,0:T(8,128)} %copy-done.7) | copy-start | bytes 4718596
  170.2 6.1 %copy-start.10 = (f32[1024,384]{1,0:T(8,128)S(1)}, f32[1024,384]{1,0:T(8,128)}, u32[]{:S(2)}) copy-start(f32[1024,384]{1,0:T(8,128)} %copy-done.9) | copy-start | bytes 4718596
Sparse Core Ops, SparseCore 0:
  19.0 126.5 all-gather.3
  164.2 147.1 reduce-scatter.1
